TPU v7x, 512 devices: a whole 4x4x16 slice. The times are simulated.
512 devices in a mesh: strip: 512 (over z, y, x, core).
Axes of the slice: x: 4, y: 4, z: 16, core: 2. Of those that a mesh axis runs over, the one named last changes fastest.
Arguments:
- velocity: float32 [2, 128, 2048, 768], P(None, None, 'strip'), may hold values from -100 to 100
Outputs:
- spatial_modes: float32 [128, 2048, 768], P(None, 'strip')
- triangle: float32 [128, 128], replicated
All inputs are finite; a program needn't handle non-finite values.
Results may differ from a plain program's by a relative error of at most 0.000094.
Values sent between devices are 32-bit elements; how exact they have to be, the bound alone decides.
No kernel may reach another device: no remote copies, remote signals or barrier semaphores. Data moves between devices by JAX's collectives and lax.ppermute only.
A program may use at most 128 MiB of HBM per device.

v0:
```python
import jax
import jax.numpy as jnp
from jax import lax
from jax.sharding import PartitionSpec as P


def extended(array, sides, width):
    for axis, dim in sides:
        size, length = (lax.axis_size(axis), array.shape[dim])
        up = [(i, (i + 1) % size) for i in range(size)]
        down = [(j, i) for i, j in up]
        last = lax.slice_in_dim(array, length - width, length, axis=dim)
        initial = lax.slice_in_dim(array, 0, width, axis=dim)
        before = lax.ppermute(last, axis, up)
        after = lax.ppermute(initial, axis, down)
        array = jnp.concatenate([before, array, after], axis=dim)
    return array


def along_second(field):
    return (
        8.0 * (jnp.roll(field, -1, 2) - jnp.roll(field, 1, 2))
        - (jnp.roll(field, -2, 2) - jnp.roll(field, 2, 2))
    ) / 12.0


def stencil_rows(padded, row_count):
    return 8.0 * (padded[:, 3 : row_count + 3] - padded[:, 1 : row_count + 1]) - (
        padded[:, 4 : row_count + 4] - padded[:, 0:row_count]
    )


def local(velocity):
    snap_count = velocity.shape[1]
    row_count = velocity.shape[2]
    col_count = velocity.shape[3]
    total_cells = row_count * lax.axis_size("strip") * col_count
    comp_u = velocity[0]
    comp_v = velocity[1]
    padded = extended(comp_v, (("strip", 1),), 2)
    v_first = stencil_rows(padded, row_count) / 12.0
    vorticity = v_first - along_second(comp_u)
    flattened = vorticity.reshape(snap_count, row_count * col_count)
    local_gram = (
        jnp.dot(
            flattened,
            flattened.T,
            precision=lax.Precision.HIGHEST,
            preferred_element_type=jnp.float32,
        )
        / total_cells
    )
    gram = lax.psum(local_gram, "strip")
    lower = jnp.linalg.cholesky(gram)
    identity = jnp.eye(snap_count, dtype=jnp.float32)
    inverse_lower = lax.linalg.triangular_solve(lower, identity, left_side=True, lower=True)
    spatial_modes = jnp.dot(
        inverse_lower,
        flattened,
        precision=lax.Precision.HIGHEST,
        preferred_element_type=jnp.float32,
    )
    return (spatial_modes.reshape(snap_count, row_count, col_count), lower.T)


def solution(mesh):
    return jax.shard_map(
        local,
        mesh=mesh,
        in_specs=(P(None, None, "strip", None),),
        out_specs=(P(None, "strip", None), P()),
        check_vma=False,
    )
```

profile of v0, /device:TPU:1, one launch (start us, length us, event | category | flops | bytes accessed | tf_op | source)
XLA Modules:
  0.0 519.4 jit_solution(6703230414431210953)
XLA Ops:
  7.2 0.0 all-reduce.2.cloned.1.call-start
  7.2 2.4 slice_bitcast_fusion
  9.6 0.6 fusion.26
  10.2 8.8 %collective-permute-start = (f32[128,2,768]{2,1,0:T(2,128)S(1)}, f32[128,2,768]{2,1,0:T(2,128)S(1)}, u32[]{:S(2)}, u32[]{:S(2)}) collective-permute-start(f32[128,2,768]{2,1,0:T(2,128)S(1)} %get-tuple-element.14), channel_id=1, source_target_pairs={{1,0},{2,1},{3,2},{4,3},{5,4},{6,5},{7,6},{8,7},{9,8},{10,9},{11,1... | collective-permute-start | bytes 2359304 | tf_op jit(solution)/shard_map/ppermute | solution.py:15
  19.0 1.9 collective-permute-start.1
  21.0 0.2 fusion.24
  21.2 0.2 fusion.22
  21.4 0.9 fusion.25
  22.3 0.9 fusion.23
  23.2 1.2 collective-permute-done
  24.4 6.5 %collective-permute-done.1 = f32[128,2,768]{2,1,0:T(2,128)S(1)} collective-permute-done((f32[128,2,768]{2,1,0:T(2,128)S(1)}, f32[128,2,768]{2,1,0:T(2,128)S(1)}, u32[]{:S(2)}, u32[]{:S(2)}) %collective-permute-start.1) | collective-permute-done | bytes 786464 | tf_op jit(solution)/shard_map/ppermute | solution.py:14
  30.9 5.1 fusion.5
  36.0 2.3 fusion.16
  38.3 0.0 all-reduce.2.cloned.1.call-update
  38.3 0.3 copy.12
  38.6 0.5 copy.7
  39.1 444.1 %all-reduce.2.cloned.1.call-done = f32[128,128]{0,1:T(8,128)} async-done(((f32[128,128]{0,1:T(8,128)}), f32[128,128]{0,1:T(8,128)}) %all-reduce.2.cloned.1.call-update) | async-done | bytes 65552 | tf_op jit(solution)/shard_map/psum | solution.py:53
  483.2 0.9 copy.6
  484.1 0.9 fusion.20
  485.0 11.7 %cholesky.17 = f32[128,128]{1,0:T(8,128)S(1)} custom-call(f32[128,128]{1,0:T(8,128)S(1)} %fusion.20), custom_call_target="Cholesky" | custom-call | tf_op jit(solution)/shard_map/jit(cholesky)/cholesky | solution.py:54
  496.8 0.6 compare_reduce_fusion
  497.4 0.7 fusion.21
  498.1 9.8 %custom-call.6 = f32[1,128,128]{1,2,0:T(8,128)S(1)} custom-call(f32[1,128,128]{2,1,0:T(8,128)S(1)} %get-tuple-element.17), custom_call_target="InvertDiagBlocksLowerTriangular" | custom-call | tf_op jit(solution)/shard_map/triangular_solve | solution.py:56
  507.9 0.2 convolution_bitcast_fusion
  508.1 1.5 fusion.27
  509.6 2.2 copy.8
  511.8 0.7 copy.9
  (1 shorter events, 0.0 us)
Async XLA Ops:
  7.2 476.1 %all-reduce.2.cloned.1.call-start = ((), (), s32[]{:S(2)}) async-start(), calls=%async_computation | async-start | bytes 131072 | tf_op jit(solution)/shard_map/psum | solution.py:53
  10.2 14.2 %collective-permute-start = (f32[128,2,768]{2,1,0:T(2,128)S(1)}, f32[128,2,768]{2,1,0:T(2,128)S(1)}, u32[]{:S(2)}, u32[]{:S(2)}) collective-permute-start(f32[128,2,768]{2,1,0:T(2,128)S(1)} %get-tuple-element.14), channel_id=1, source_target_pairs={{1,0},{2,1},{3,2},{4,3},{5,4},{6,5},{7,6},{8,7},{9,8},{10,9},{11,1... | collective-permute-start | bytes 2359304 | tf_op jit(solution)/shard_map/ppermute | solution.py:15
  19.0 11.9 %collective-permute-start.1 = (f32[128,2,768]{2,1,0:T(2,128)S(1)}, f32[128,2,768]{2,1,0:T(2,128)S(1)}, u32[]{:S(2)}, u32[]{:S(2)}) collective-permute-start(f32[128,2,768]{2,1,0:T(2,128)S(1)} %get-tuple-element.15), channel_id=1, source_target_pairs={{0,1},{1,2},{2,3},{3,4},{4,5},{5,6},{6,7},{7,8},{8,9},{9,10},{10,1... | collective-permute-start | bytes 2359304 | tf_op jit(solution)/shard_map/ppermute | solution.py:14
Sparse Core Ops, SparseCore 0:
  38.5 444.7 all-reduce.1
where the time goes:
time: 520 us; the launch traced here: 519 us
  waiting for transfers between devices  452 us (87%)
  other arithmetic  28.8 us (6%)
  between operations  14.1 us (3%)
  starting transfers between devices  10.7 us (2%)
  local copies, waits for them, and re-layouts  9.79 us (2%)
    psum x1, waiting for transfers between devices, local(): gram = lax.psum(local_gram, 'strip')  444 us
    another operation x3, other arithmetic, local(): lower = jnp.linalg.cholesky(gram)  12.4 us
  transfers between devices with their start and end apart: 3, of which 3 were waited for; matrix products, arithmetic and copies ran while one was open for 1% of the time, Pallas kernels for 0%

commit v1 on v0

--- a/solution.py
+++ b/solution.py
@@ -50,7 +50,7 @@
         )
         / total_cells
     )
-    gram = lax.psum(local_gram, "strip")
+    gram = jnp.sum(lax.all_gather(local_gram, "strip"), axis=0)
     lower = jnp.linalg.cholesky(gram)
     identity = jnp.eye(snap_count, dtype=jnp.float32)
     inverse_lower = lax.linalg.triangular_solve(lower, identity, left_side=True, lower=True)

time: 520 us -> 329 us (0.63)
  waiting for transfers between devices: 452 us -> 250 us
  other arithmetic: 28.8 us -> 41 us
    psum x1 -> x0, waiting for transfers between devices: 444 us -> none  [local(): gram = lax.psum(local_gram, 'strip')]
    all_gather x0 -> x1, waiting for transfers between devices: none -> 242 us  [local(): gram = jnp.sum(lax.all_gather(local_gram, 'strip'), axis=0)]
    reduce_sum x0 -> x1, other arithmetic: none -> 13.3 us  [local(): gram = jnp.sum(lax.all_gather(local_gram, 'strip'), axis=0)]
where the time goes in v1:
time: 329 us
  waiting for transfers between devices  250 us (76%)
  other arithmetic  41 us (12%)
  between operations  14.1 us (4%)
  starting transfers between devices  10.7 us (3%)
  local copies, waits for them, and re-layouts  8.95 us (3%)
  matrix products  4.07 us (1%)
    all_gather x1, waiting for transfers between devices, local(): gram = jnp.sum(lax.all_gather(local_gram, 'strip'), axis=0)  242 us
    reduce_sum x1, other arithmetic, local(): gram = jnp.sum(lax.all_gather(local_gram, 'strip'), axis=0)  13.3 us
    another operation x3, other arithmetic, local(): lower = jnp.linalg.cholesky(gram)  12.4 us
    another operation x1, other arithmetic, local(): lax.linalg.triangular_solve(lower, identity, left_side=True, lower=True)  9.81 us
    ppermute x1, starting transfers between devices, extended(): after = lax.ppermute(initial, axis, down)  8.79 us
  transfers between devices with their start and end apart: 3, of which 3 were waited for; matrix products, arithmetic and copies ran while one was open for 1% of the time, Pallas kernels for 0%

profile of v1, /device:TPU:1, one launch (start us, length us, event | category | flops | bytes accessed | tf_op | source)
XLA Modules:
  0.0 328.6 jit_solution(2331024837784504634)
XLA Ops:
  7.2 0.0 all-gather.3.cloned.1.call-start
  7.2 2.4 slice_bitcast_fusion
  9.6 0.6 fusion.26
  10.2 8.8 %collective-permute-start = (f32[128,2,768]{2,1,0:T(2,128)S(1)}, f32[128,2,768]{2,1,0:T(2,128)S(1)}, u32[]{:S(2)}, u32[]{:S(2)}) collective-permute-start(f32[128,2,768]{2,1,0:T(2,128)S(1)} %get-tuple-element.16), channel_id=1, source_target_pairs={{1,0},{2,1},{3,2},{4,3},{5,4},{6,5},{7,6},{8,7},{9,8},{10,9},{11,1... | collective-permute-start | bytes 2359304 | tf_op jit(solution)/shard_map/ppermute | solution.py:15
  19.0 1.9 collective-permute-start.1
  21.0 0.2 fusion.24
  21.2 0.2 fusion.22
  21.4 0.9 fusion.25
  22.3 0.9 fusion.23
  23.2 1.2 collective-permute-done
  24.4 6.5 %collective-permute-done.1 = f32[128,2,768]{2,1,0:T(2,128)S(1)} collective-permute-done((f32[128,2,768]{2,1,0:T(2,128)S(1)}, f32[128,2,768]{2,1,0:T(2,128)S(1)}, u32[]{:S(2)}, u32[]{:S(2)}) %collective-permute-start.1) | collective-permute-done | bytes 786464 | tf_op jit(solution)/shard_map/ppermute | solution.py:14
  30.9 4.9 %fusion.5 = f32[128,4,768]{2,1,0:T(4,128)S(1)} fusion(f32[128,2,768]{2,1,0:T(2,128)S(1)} %collective-permute-done.1, f32[128,4,768]{2,1,0:T(4,128)S(1)} %get-tuple-element.7, f32[128,2,768]{2,1,0:T(2,128)S(1)} %collective-permute-done, f32[128,4,1]{2,1,0:T(4,128)S(1)} %get-tuple-element.13, f32[128,4,767]{2,1,0:T(4,128)S(1)} %get-tuple-element.15, ...), kind=kLoop, calls=%fused_computation.9 | loop fusion | flops 7471104 | bytes 11010048 | tf_op jit(solution)/shard_map/sub | solution.py:42
  35.8 2.3 fusion.16
  38.1 0.0 all-gather.3.cloned.1.call-update
  38.2 0.3 copy.15
  38.5 0.5 copy.12
  38.9 241.9 %all-gather.3.cloned.1.call-done = f32[65536,128]{1,0:T(8,128)} async-done(((f32[128,128]{1,0:T(8,128)}), f32[65536,128]{1,0:T(8,128)}) %all-gather.3.cloned.1.call-update) | async-done | bytes 33554448 | tf_op jit(solution)/shard_map/all_gather | solution.py:53
  280.8 13.3 %reduce_sum.9 = f32[128,128]{1,0:T(8,128)S(1)} reduce(f32[512,128,128]{2,1,0:T(8,128)} %bitcast.29, f32[]{:T(128)} %constant.47.clone.1), dimensions={0}, to_apply=%region_0.1 | reduce | flops 8372224 | bytes 33619972 | tf_op jit(solution)/shard_map/reduce_sum | solution.py:53
  294.1 0.1 copy.11
  294.2 11.7 %cholesky.17 = f32[128,128]{1,0:T(8,128)S(1)} custom-call(f32[128,128]{1,0:T(8,128)S(1)} %fusion.20), custom_call_target="Cholesky" | custom-call | tf_op jit(solution)/shard_map/jit(cholesky)/cholesky | solution.py:54
  306.0 0.6 compare_reduce_fusion
  306.6 0.7 fusion.21
  307.3 0.7 copy.14
  308.0 9.8 %custom-call.6 = f32[1,128,128]{1,2,0:T(8,128)S(1)} custom-call(f32[1,128,128]{2,1,0:T(8,128)S(1)} %get-tuple-element.19), custom_call_target="InvertDiagBlocksLowerTriangular" | custom-call | tf_op jit(solution)/shard_map/triangular_solve | solution.py:56
  317.8 0.2 convolution_bitcast_fusion
  318.1 1.5 fusion.27
  319.6 2.2 copy.13
  (2 shorter events, 0.0 us)
Async XLA Ops:
  7.2 273.7 %all-gather.3.cloned.1.call-start = ((), (), s32[]{:S(2)}) async-start(), calls=%async_computation | async-start | bytes 33619968 | tf_op jit(solution)/shard_map/all_gather | solution.py:53
  10.2 14.2 %collective-permute-start = (f32[128,2,768]{2,1,0:T(2,128)S(1)}, f32[128,2,768]{2,1,0:T(2,128)S(1)}, u32[]{:S(2)}, u32[]{:S(2)}) collective-permute-start(f32[128,2,768]{2,1,0:T(2,128)S(1)} %get-tuple-element.16), channel_id=1, source_target_pairs={{1,0},{2,1},{3,2},{4,3},{5,4},{6,5},{7,6},{8,7},{9,8},{10,9},{11,1... | collective-permute-start | bytes 2359304 | tf_op jit(solution)/shard_map/ppermute | solution.py:15
  19.0 11.9 %collective-permute-start.1 = (f32[128,2,768]{2,1,0:T(2,128)S(1)}, f32[128,2,768]{2,1,0:T(2,128)S(1)}, u32[]{:S(2)}, u32[]{:S(2)}) collective-permute-start(f32[128,2,768]{2,1,0:T(2,128)S(1)} %get-tuple-element.17), channel_id=1, source_target_pairs={{0,1},{1,2},{2,3},{3,4},{4,5},{5,6},{6,7},{7,8},{8,9},{9,10},{10,1... | collective-permute-start | bytes 2359304 | tf_op jit(solution)/shard_map/ppermute | solution.py:14
Sparse Core Ops, SparseCore 0:
  38.3 242.4 all-gather.2
